TPU v7x, 512 devices: a whole 4x8x8 slice. The times are simulated.
512 devices in a mesh: worker: 16 (over x, z_lo, core), fsdp: 32 (over z_hi, y).
Axes of the slice: x: 4, y: 8, z: 8 (z_hi: 4, z_lo: 2; z = z_hi * 2 + z_lo), core: 2. Of those that a mesh axis runs over, the one named last changes fastest.
Arguments:
- hidden: bfloat16 [9472, 65536], P('fsdp', 'worker'), may hold values from -6 to 6
- cotangent: bfloat16 [65536, 1792], P(('worker', 'fsdp')), may hold values from -6 to 6
- first_moment: bfloat16 [16, 9472, 1792], P('worker', 'fsdp'), may hold values from -0.0625 to 0.0625
- second_moment: bfloat16 [16, 9472, 1792], P('worker', 'fsdp'), may hold values from 1.21593475e-05 to 0.00024414062
- outer_momentum: bfloat16 [9472, 1792], P('fsdp', 'worker'), may hold values from -4 to 4
Outputs:
- new_momentum: float32 [9472, 1792], P('fsdp', 'worker')
All inputs are finite; a program needn't handle non-finite values.
Results may differ from a plain program's by a relative error of at most 0.0003.
Values may be sent and summed in bfloat16 or wider, within the bound.
No kernel may reach another device: no remote copies, remote signals or barrier semaphores. Data moves between devices by JAX's collectives and lax.ppermute only.
A program may use at most 64 MiB of HBM per device.

v0:
```python
import jax
import jax.numpy as jnp
from jax import lax
from jax.sharding import PartitionSpec as P


def shards(hidden, cotangent, first_moment, second_moment, outer_momentum):
    gathered = lax.all_gather(cotangent, "fsdp", axis=0, tiled=True)
    gradient = jnp.dot(hidden, gathered, preferred_element_type=jnp.float32) / gathered.shape[0]
    first_new = 0.9 * first_moment[0].astype(jnp.float32) + 0.1 * gradient
    second_new = 0.95 * second_moment[0].astype(jnp.float32) + 0.05 * gradient * gradient
    pseudo = first_new / (jnp.sqrt(second_new) + 1e-08)
    summed = lax.psum_scatter(pseudo, "worker", scatter_dimension=1, tiled=True)
    average = summed / lax.axis_size("worker")
    return 0.9 * outer_momentum.astype(jnp.float32) + average


def solution(mesh):
    in_specs = (
        P("fsdp", "worker"),
        P(("worker", "fsdp"), None),
        P("worker", "fsdp", None),
        P("worker", "fsdp", None),
        P("fsdp", "worker"),
    )
    out_specs = P("fsdp", "worker")
    return jax.shard_map(shards, mesh=mesh, in_specs=in_specs, out_specs=out_specs, check_vma=False)
```

profile of v0, /device:TPU:1, one launch (start us, length us, event | category | flops | bytes accessed | tf_op | source)
XLA Modules:
  0.0 304.3 jit_solution(2699673919500388459)
XLA Ops:
  6.5 0.0 copy-start
  6.5 0.0 all-gather.2.cloned.1.call-start
  6.5 0.7 all-gather.2.cloned.1.call-update
  7.3 0.0 reduce-scatter.4.cloned.1.call-start
  7.3 184.0 %all-gather.2.cloned.1.call-done = bf16[4096,1792]{1,0:T(8,128)(2,1)} async-done(((bf16[128,1792]{1,0:T(8,128)(2,1)}), bf16[4096,1792]{1,0:T(8,128)(2,1)}) %all-gather.2.cloned.1.call-update) | async-done | bytes 14680080 | tf_op jit(solution)/shard_map/all_gather | solution.py:8
  191.4 0.0 copy-done
  191.4 12.5 %fusion.2 = f32[296,1792]{1,0:T(8,128)} fusion(bf16[1,296,1792]{2,1,0:T(8,128)(2,1)} %param.8, bf16[1,296,1792]{2,1,0:T(8,128)(2,1)} %param.7, bf16[296,4096]{1,0:T(8,128)(2,1)S(1)} %copy-done, bf16[4096,1792]{1,0:T(8,128)(2,1)} %all-gather.2.cloned.1.call-done), kind=kOutput, calls=%fused_computation.3 | convolution fusion | flops 4351664128 | bytes 21348352 | tf_op jit(solution)/shard_map/dot_general | solution.py:9
  203.9 3.2 %copy.6 = f32[296,1792]{0,1:T(8,128)} copy(f32[296,1792]{1,0:T(8,128)} %fusion.2) | data formatting | bytes 4243456
  207.1 0.0 copy-start.1
  207.1 0.0 reduce-scatter.4.cloned.1.call-update
  207.1 88.6 %reduce-scatter.4.cloned.1.call-done = f32[112,296]{1,0:T(8,128)} async-done(((f32[1792,296]{1,0:T(8,128)}), f32[112,296]{1,0:T(8,128)}) %reduce-scatter.4.cloned.1.call-update) | async-done | bytes 132624
  295.7 1.0 copy.7
  296.8 0.0 copy-done.1
  296.8 0.7 multiply_add_fusion
Async XLA Ops:
  6.5 184.8 %copy-start = (bf16[296,4096]{1,0:T(8,128)(2,1)S(1)}, bf16[296,4096]{1,0:T(8,128)(2,1)}, u32[]{:S(2)}) copy-start(bf16[296,4096]{1,0:T(8,128)(2,1)} %param.5) | copy-start | bytes 7274500
  6.5 184.8 %all-gather.2.cloned.1.call-start = ((), (), s32[]{:S(2)}) async-start(), calls=%async_computation.1 | async-start | bytes 15138816 | tf_op jit(solution)/shard_map/all_gather | solution.py:8
  7.3 288.5 %reduce-scatter.4.cloned.1.call-start = ((), (), s32[]{:S(2)}) async-start(), calls=%async_computation.2 | async-start | bytes 2924544
  207.1 89.7 %copy-start.1 = (bf16[296,112]{1,0:T(8,128)(2,1)S(1)}, bf16[296,112]{1,0:T(8,128)(2,1)}, u32[]{:S(2)}) copy-start(bf16[296,112]{1,0:T(8,128)(2,1)} %param.9) | copy-start | bytes 198916
Sparse Core Ops, SparseCore 0:
  10.5 180.7 all-gather.1
  207.2 88.4 reduce-scatter.3
where the time goes:
time: 306 us; the launch traced here: 304 us
  waiting for transfers between devices  273 us (89%)
  between operations  13.4 us (4%)
  matrix products  12.5 us (4%)
  local copies, waits for them, and re-layouts  4.24 us (1%)
    all_gather x1, waiting for transfers between devices, shards(): gathered = lax.all_gather(cotangent, 'fsdp', axis=0, tiled=True)  184 us
    unnamed x3, waiting for transfers between devices  89.4 us
    dot_general x1, matrix products, shards(): jnp.dot(hidden, gathered, preferred_element_type=jnp.float32)  12.5 us
  transfers between devices with their start and end apart: 2, of which 2 were waited for; matrix products, arithmetic and copies ran while one was open for 0% of the time, Pallas kernels for 0%

commit v1 on v0

v1 whole, which is shorter than its diff:
```python
import jax
import jax.numpy as jnp
from jax import lax
from jax.sharding import Mesh
from jax.sharding import PartitionSpec as P

W = ("wx", "wz", "wc")
F = ("fz", "fy")


def shards(hidden, cotangent, first_moment, second_moment, outer_momentum):
    gathered = lax.all_gather(cotangent, "fy", axis=0, tiled=True)
    gathered = lax.all_gather(gathered, "fz", axis=0, tiled=True)
    gradient = jnp.dot(hidden, gathered, preferred_element_type=jnp.float32) / gathered.shape[0]
    first_new = 0.9 * first_moment[0].astype(jnp.float32) + 0.1 * gradient
    second_new = 0.95 * second_moment[0].astype(jnp.float32) + 0.05 * gradient * gradient
    pseudo = first_new / (jnp.sqrt(second_new) + 1e-08)
    summed = lax.psum_scatter(pseudo, "wx", scatter_dimension=1, tiled=True)
    summed = lax.psum_scatter(summed, "wz", scatter_dimension=1, tiled=True)
    summed = lax.psum_scatter(summed, "wc", scatter_dimension=1, tiled=True)
    average = summed / 16
    return 0.9 * outer_momentum.astype(jnp.float32) + average


def solution(mesh):
    sizes = {"worker": (4, 2, 2), "fsdp": (4, 8)}
    fine = Mesh(mesh.devices.reshape(sizes["worker"] + sizes["fsdp"]), W + F)
    in_specs = (
        P(F, W),
        P(W + F, None),
        P(W, F, None),
        P(W, F, None),
        P(F, W),
    )
    out_specs = P(F, W)
    return jax.shard_map(shards, mesh=fine, in_specs=in_specs, out_specs=out_specs, check_vma=False)
```

time: 306 us -> 441 us (1.44)
  waiting for transfers between devices: 273 us -> 410 us
    all_gather x1 -> x2, waiting for transfers between devices: 184 us -> 323 us  [the longest x1 263 us: shards(): gathered = lax.all_gather(gathered, 'fz', axis=0, tiled=True)]
    unnamed x3 -> x8, waiting for transfers between devices: 89.4 us -> 87.1 us
  transfers between devices with their start and end apart: 2 -> 5, of which waited for: 2 -> 5; matrix products, arithmetic and copies ran while one was open for 0% -> 0% of each run, Pallas kernels for 0% -> 0%
where the time goes in v1:
time: 441 us
  waiting for transfers between devices  410 us (93%)
  between operations  13.2 us (3%)
  matrix products  12.5 us (3%)
    all_gather x1, waiting for transfers between devices, shards(): gathered = lax.all_gather(gathered, 'fz', axis=0, tiled=True)  263 us
    unnamed x8, waiting for transfers between devices  87.1 us
    all_gather x1, waiting for transfers between devices, shards(): gathered = lax.all_gather(cotangent, 'fy', axis=0, tiled=True)  59.6 us
    dot_general x1, matrix products, shards(): jnp.dot(hidden, gathered, preferred_element_type=jnp.float32)  12.5 us
  transfers between devices with their start and end apart: 5, of which 5 were waited for; matrix products, arithmetic and copies ran while one was open for 0% of the time, Pallas kernels for 0%

profile of v1, /device:TPU:1, one launch (start us, length us, event | category | flops | bytes accessed | tf_op | source)
XLA Modules:
  0.0 440.6 jit_solution(18052096988505240915)
XLA Ops:
  6.5 0.0 copy-start
  6.5 0.0 all-gather.3.cloned.1.call-start
  6.5 0.7 all-gather.3.cloned.1.call-update
  7.3 0.0 all-gather.5.cloned.1.call-start
  7.3 59.6 %all-gather.3.cloned.1.call-done = bf16[1024,1792]{1,0:T(8,128)(2,1)} async-done(((bf16[128,1792]{1,0:T(8,128)(2,1)}), bf16[1024,1792]{1,0:T(8,128)(2,1)}) %all-gather.3.cloned.1.call-update) | async-done | bytes 3670032 | tf_op jit(solution)/shard_map/all_gather | solution.py:12
  66.9 0.0 all-gather.5.cloned.1.call-update
  66.9 0.0 reduce-scatter.10.cloned.1.call-start
  67.0 263.2 %all-gather.5.cloned.1.call-done = bf16[4096,1792]{1,0:T(8,128)(2,1)} async-done(((bf16[1024,1792]{1,0:T(8,128)(2,1)}), bf16[4096,1792]{1,0:T(8,128)(2,1)}) %all-gather.5.cloned.1.call-update) | async-done | bytes 14680080 | tf_op jit(solution)/shard_map/all_gather | solution.py:13
  330.2 0.0 copy-done
  330.2 12.5 %fusion.2 = f32[296,1792]{1,0:T(8,128)} fusion(bf16[1,296,1792]{2,1,0:T(8,128)(2,1)} %param.8, bf16[1,296,1792]{2,1,0:T(8,128)(2,1)} %param.7, bf16[296,4096]{1,0:T(8,128)(2,1)S(1)} %copy-done, bf16[4096,1792]{1,0:T(8,128)(2,1)} %all-gather.5.cloned.1.call-done), kind=kOutput, calls=%fused_computation.3 | convolution fusion | flops 4351664128 | bytes 21348352 | tf_op jit(solution)/shard_map/dot_general | solution.py:14
  342.7 3.2 copy.6
  345.9 0.0 copy-start.1
  345.9 0.0 reduce-scatter.10.cloned.1.call-update
  345.9 0.0 reduce-scatter.12.cloned.1.call-start
  346.0 38.9 %reduce-scatter.10.cloned.1.call-done = f32[448,296]{1,0:T(8,128)} async-done(((f32[1792,296]{1,0:T(8,128)}), f32[448,296]{1,0:T(8,128)}) %reduce-scatter.10.cloned.1.call-update) | async-done | bytes 530448
  384.9 0.0 reduce-scatter.12.cloned.1.call-update
  384.9 0.0 reduce-scatter.14.cloned.1.call-start
  384.9 26.8 %reduce-scatter.12.cloned.1.call-done = f32[224,296]{1,0:T(8,128)} async-done(((f32[448,296]{1,0:T(8,128)}), f32[224,296]{1,0:T(8,128)}) %reduce-scatter.12.cloned.1.call-update) | async-done | bytes 265232
  411.7 0.0 reduce-scatter.14.cloned.1.call-update
  411.7 20.6 %reduce-scatter.14.cloned.1.call-done = f32[112,296]{1,0:T(8,128)} async-done(((f32[224,296]{1,0:T(8,128)}), f32[112,296]{1,0:T(8,128)}) %reduce-scatter.14.cloned.1.call-update) | async-done | bytes 132624
  432.3 1.0 copy.11
  433.3 0.0 copy-done.1
  433.4 0.7 multiply_add_fusion
Async XLA Ops:
  6.5 323.6 %copy-start = (bf16[296,4096]{1,0:T(8,128)(2,1)S(1)}, bf16[296,4096]{1,0:T(8,128)(2,1)}, u32[]{:S(2)}) copy-start(bf16[296,4096]{1,0:T(8,128)(2,1)} %param.5) | copy-start | bytes 7274500
  6.5 60.4 %all-gather.3.cloned.1.call-start = ((), (), s32[]{:S(2)}) async-start(), calls=%async_computation.3 | async-start | bytes 4128768 | tf_op jit(solution)/shard_map/all_gather | solution.py:12
  7.3 322.9 %all-gather.5.cloned.1.call-start = ((), (), s32[]{:S(2)}) async-start(), calls=%async_computation.4 | async-start | bytes 18350080 | tf_op jit(solution)/shard_map/all_gather | solution.py:13
  66.9 317.9 %reduce-scatter.10.cloned.1.call-start = ((), (), s32[]{:S(2)}) async-start(), calls=%async_computation.5 | async-start | bytes 3440640
  345.9 87.5 %copy-start.1 = (bf16[296,112]{1,0:T(8,128)(2,1)S(1)}, bf16[296,112]{1,0:T(8,128)(2,1)}, u32[]{:S(2)}) copy-start(bf16[296,112]{1,0:T(8,128)(2,1)} %param.9) | copy-start | bytes 198916
  345.9 65.8 %reduce-scatter.12.cloned.1.call-start = ((), (), s32[]{:S(2)}) async-start(), calls=%async_computation.6 | async-start | bytes 1032192
  384.9 47.4 %reduce-scatter.14.cloned.1.call-start = ((), (), s32[]{:S(2)}) async-start(), calls=%async_computation.7 | async-start | bytes 516096
Sparse Core Ops, SparseCore 0:
  9.4 57.4 all-gather.2
  69.0 261.1 all-gather.4
  346.0 38.7 reduce-scatter.9
  387.5 24.1 reduce-scatter.11
  414.3 17.9 reduce-scatter.13

commit v2 on v0

--- a/solution.py
+++ b/solution.py
@@ -10,8 +10,11 @@
     first_new = 0.9 * first_moment[0].astype(jnp.float32) + 0.1 * gradient
     second_new = 0.95 * second_moment[0].astype(jnp.float32) + 0.05 * gradient * gradient
     pseudo = first_new / (jnp.sqrt(second_new) + 1e-08)
-    summed = lax.psum_scatter(pseudo, "worker", scatter_dimension=1, tiled=True)
-    average = summed / lax.axis_size("worker")
+    workers = lax.axis_size("worker")
+    rows, cols = pseudo.shape
+    blocks = pseudo.reshape(rows, workers, cols // workers)
+    received = lax.all_to_all(blocks, "worker", 1, 1, tiled=True)
+    average = received.sum(axis=1) / workers
     return 0.9 * outer_momentum.astype(jnp.float32) + average
 
 

time: 306 us -> 279 us (0.912)
  waiting for transfers between devices: 273 us -> 185 us
  blocking collectives: 0 us -> 59.1 us
    unnamed x3 -> x1, waiting for transfers between devices: 89.4 us -> 0.71 us
    all_to_all x0 -> x1, blocking collectives: none -> 59.1 us  [shards(): received = lax.all_to_all(blocks, 'worker', 1, 1, tiled=True)]
    reshape x0 -> x2, local copies, waits for them, and re-layouts: none -> 6.41 us  [shards(): blocks = pseudo.reshape(rows, workers, cols // workers)]
    unnamed x6 -> x4, local copies, waits for them, and re-layouts: 4.24 us -> 0.01 us
  transfers between devices with their start and end apart: 2 -> 1, of which waited for: 2 -> 1; matrix products, arithmetic and copies ran while one was open for 0% -> 0% of each run, Pallas kernels for 0% -> 0%
where the time goes in v2:
time: 279 us
  waiting for transfers between devices  185 us (66%)
  blocking collectives  59.1 us (21%)
  between operations  13.4 us (5%)
  matrix products  12.5 us (4%)
  local copies, waits for them, and re-layouts  6.42 us (2%)
    all_gather x1, waiting for transfers between devices, shards(): gathered = lax.all_gather(cotangent, 'fsdp', axis=0, tiled=True)  184 us
    all_to_all x1, blocking collectives, shards(): received = lax.all_to_all(blocks, 'worker', 1, 1, tiled=True)  59.1 us
    dot_general x1, matrix products, shards(): jnp.dot(hidden, gathered, preferred_element_type=jnp.float32)  12.5 us
    reshape x2, local copies, waits for them, and re-layouts, shards(): blocks = pseudo.reshape(rows, workers, cols // workers)  6.41 us
  transfers between devices with their start and end apart: 1, of which 1 were waited for; matrix products, arithmetic and copies ran while one was open for 0% of the time, Pallas kernels for 0%

profile of v2, /device:TPU:1, one launch (start us, length us, event | category | flops | bytes accessed | tf_op | source)
XLA Modules:
  0.0 278.8 jit_solution(10959432336809336310)
XLA Ops:
  6.5 0.0 copy-start
  6.5 0.0 all-gather.2.cloned.1.call-start
  6.5 0.7 all-gather.2.cloned.1.call-update
  7.3 184.1 %all-gather.2.cloned.1.call-done = bf16[4096,1792]{1,0:T(8,128)(2,1)} async-done(((bf16[128,1792]{1,0:T(8,128)(2,1)}), bf16[4096,1792]{1,0:T(8,128)(2,1)}) %all-gather.2.cloned.1.call-update) | async-done | bytes 14680080 | tf_op jit(solution)/shard_map/all_gather | solution.py:8
  191.4 0.0 copy-done
  191.4 12.5 %fusion.2 = f32[296,1792]{1,0:T(8,128)} fusion(bf16[1,296,1792]{2,1,0:T(8,128)(2,1)} %param.8, bf16[1,296,1792]{2,1,0:T(8,128)(2,1)} %param.7, bf16[296,4096]{1,0:T(8,128)(2,1)S(1)} %copy-done, bf16[4096,1792]{1,0:T(8,128)(2,1)} %all-gather.2.cloned.1.call-done), kind=kOutput, calls=%fused_computation.3 | convolution fusion | flops 4351664128 | bytes 21348352 | tf_op jit(solution)/shard_map/dot_general | solution.py:9
  203.9 3.9 %reshape.9 = f32[296,16,112]{2,1,0:T(8,128)} reshape(f32[296,1792]{1,0:T(8,128)} %fusion.2) | data formatting | bytes 4243456 | tf_op jit(solution)/shard_map/reshape | solution.py:15
  207.8 2.5 copy.6
  210.3 59.1 %all_to_all.5 = f32[296,16,112]{2,0,1:T(8,128)} all-to-all(f32[296,16,112]{2,0,1:T(8,128)S(1)} %copy.6), channel_id=1, replica_groups=mesh['worker'=16,'fsdp'=32] {'worker'}, dimensions={1} | all-to-all | bytes 4243456 | tf_op jit(solution)/shard_map/all_to_all | solution.py:16
  269.4 0.0 copy-start.1
  269.4 1.9 reduce_sum.9
  271.3 0.0 copy-done.1
  271.3 0.7 multiply_add_fusion
Async XLA Ops:
  6.5 184.8 %copy-start = (bf16[296,4096]{1,0:T(8,128)(2,1)S(1)}, bf16[296,4096]{1,0:T(8,128)(2,1)}, u32[]{:S(2)}) copy-start(bf16[296,4096]{1,0:T(8,128)(2,1)} %param.5) | copy-start | bytes 7274500
  6.5 184.8 %all-gather.2.cloned.1.call-start = ((), (), s32[]{:S(2)}) async-start(), calls=%async_computation.1 | async-start | bytes 15138816 | tf_op jit(solution)/shard_map/all_gather | solution.py:8
  269.4 1.9 copy-start.1
Sparse Core Ops, SparseCore 0:
  10.5 180.7 all-gather.1

commit v3 on v0

v3 whole, which is shorter than its diff:
```python
import jax
import jax.numpy as jnp
from jax import lax
from jax.sharding import PartitionSpec as P

CHUNKS = 2


def shards(hidden, cotangent, first_moment, second_moment, outer_momentum):
    workers = lax.axis_size("worker")
    rows = hidden.shape[0]
    tokens_here, cols = cotangent.shape
    width = cols // workers // CHUNKS
    cot = cotangent.reshape(tokens_here, workers, CHUNKS, width)
    m1 = first_moment[0].reshape(rows, workers, CHUNKS, width)
    m2 = second_moment[0].reshape(rows, workers, CHUNKS, width)
    parts = []
    for j in range(CHUNKS):
        if parts:
            hidden, m1, m2, _ = lax.optimization_barrier((hidden, m1, m2, parts[-1]))
        piece = cot[:, :, j, :].reshape(tokens_here, workers * width)
        gathered = lax.all_gather(piece, "fsdp", axis=0, tiled=True)
        gradient = jnp.dot(hidden, gathered, preferred_element_type=jnp.float32) / gathered.shape[0]
        gradient = gradient.reshape(rows, workers, width)
        first_new = 0.9 * m1[:, :, j, :].astype(jnp.float32) + 0.1 * gradient
        second_new = 0.95 * m2[:, :, j, :].astype(jnp.float32) + 0.05 * gradient * gradient
        pseudo = first_new / (jnp.sqrt(second_new) + 1e-08)
        received = lax.all_to_all(pseudo, "worker", 1, 1, tiled=True)
        parts.append(received.sum(axis=1) / workers)
    average = jnp.stack(parts, axis=1).reshape(rows, CHUNKS * width)
    return 0.9 * outer_momentum.astype(jnp.float32) + average


def solution(mesh):
    in_specs = (
        P("fsdp", "worker"),
        P(("worker", "fsdp"), None),
        P("worker", "fsdp", None),
        P("worker", "fsdp", None),
        P("fsdp", "worker"),
    )
    out_specs = P("fsdp", "worker")
    return jax.shard_map(shards, mesh=mesh, in_specs=in_specs, out_specs=out_specs, check_vma=False)
```

time: 306 us -> 336 us (1.098)
  starting transfers between devices: 0.04 us -> 13.1 us
  other arithmetic: 0.69 us -> 10.9 us
  local copies, waits for them, and re-layouts: 4.24 us -> 9.54 us
  waiting for transfers between devices: 273 us -> 277 us
    unnamed x3 -> x2, waiting for transfers between devices: 89.4 us -> 0.71 us
    all_gather x1 -> x2, waiting for transfers between devices: 184 us -> 258 us  [shards(): gathered = lax.all_gather(piece, 'fsdp', axis=0, tiled=True)]
    all_to_all x0 -> x2, waiting for transfers between devices: none -> 17.9 us  [shards(): received = lax.all_to_all(pseudo, 'worker', 1, 1, tiled=True)]
    all_to_all x0 -> x2, starting transfers between devices: none -> 13 us  [shards(): received = lax.all_to_all(pseudo, 'worker', 1, 1, tiled=True)]
    div x0 -> x4, other arithmetic: none -> 7.38 us  [the longest x2 7.36 us: shards(): pseudo = first_new / (jnp.sqrt(second_new) + 1e-08)]
    dot_general x1 -> x2, matrix products: 12.5 us -> 11.6 us  [shards(): jnp.dot(hidden, gathered, preferred_element_type=jnp.float32)]
  transfers between devices with their start and end apart: 2 -> 4, of which waited for: 2 -> 3; matrix products, arithmetic and copies ran while one was open for 0% -> 8% of each run, Pallas kernels for 0% -> 0%
where the time goes in v3:
time: 336 us
  waiting for transfers between devices  277 us (82%)
  between operations  13.5 us (4%)
  starting transfers between devices  13.1 us (4%)
  matrix products  11.6 us (3%)
  other arithmetic  10.9 us (3%)
  local copies, waits for them, and re-layouts  9.54 us (3%)
    all_gather x2, waiting for transfers between devices, shards(): gathered = lax.all_gather(piece, 'fsdp', axis=0, tiled=True)  258 us
    all_to_all x2, waiting for transfers between devices, shards(): received = lax.all_to_all(pseudo, 'worker', 1, 1, tiled=True)  17.9 us
    all_to_all x2, starting transfers between devices, shards(): received = lax.all_to_all(pseudo, 'worker', 1, 1, tiled=True)  13 us
    dot_general x2, matrix products, shards(): jnp.dot(hidden, gathered, preferred_element_type=jnp.float32)  11.6 us
    div x2, other arithmetic, shards(): pseudo = first_new / (jnp.sqrt(second_new) + 1e-08)  7.36 us
  transfers between devices with their start and end apart: 4, of which 3 were waited for; matrix products, arithmetic and copies ran while one was open for 8% of the time, Pallas kernels for 0%

profile of v3, /device:TPU:1, one launch (start us, length us, event | category | flops | bytes accessed | tf_op | source)
XLA Modules:
  0.0 335.5 jit_solution(1044207389042001825)
XLA Ops:
  6.5 0.0 copy-start
  6.5 0.0 all-gather.5.cloned.1.call-start
  6.5 1.4 copy.24
  8.0 0.8 fusion.8
  8.8 0.0 all-gather.5.cloned.1.call-update
  8.8 0.0 copy-start.1
  8.8 0.0 all-gather.3.cloned.1.call-start
  8.9 0.7 all-gather.3.cloned.1.call-update
  9.6 2.5 copy.22
  12.0 0.0 copy-done.1
  12.0 1.5 copy.26
  13.6 139.7 %all-gather.5.cloned.1.call-done = bf16[4096,896]{0,1:T(8,128)(2,1)} async-done(((bf16[128,896]{0,1:T(8,128)(2,1)}), bf16[4096,896]{0,1:T(8,128)(2,1)}) %all-gather.5.cloned.1.call-update) | async-done | bytes 7340048 | tf_op jit(solution)/shard_map/all_gather | solution.py:22
  153.3 0.0 copy-done
  153.3 5.8 %convolution_multiply_fusion = f32[296,896]{1,0:T(8,128)S(1)} fusion(bf16[296,4096]{1,0:T(8,128)(2,1)S(1)} %copy-done, bf16[4096,896]{0,1:T(8,128)(2,1)} %all-gather.5.cloned.1.call-done), kind=kOutput, calls=%fused_computation.13 | convolution fusion | flops 2172914688 | bytes 10825728 | tf_op jit(solution)/shard_map/dot_general | solution.py:23
  159.1 1.6 copy.29
  160.7 3.7 %fusion.7 = f32[296,16,56]{0,2,1:T(8,128)} fusion(f32[296,16,56]{0,2,1:T(8,128)} %bitcast.41, bf16[296,16,2,56]{0,3,2,1:T(8,128)(2,1)} %bitcast.42, bf16[296,16,2,56]{0,3,2,1:T(8,128)(2,1)} %bitcast.44), kind=kLoop, calls=%fused_computation.9 | loop fusion | flops 2917376 | bytes 3813376 | tf_op jit(solution)/shard_map/div | solution.py:27
  164.5 6.5 %all-to-all-start.1 = ((f32[296,16,56]{0,2,1:T(8,128)}), f32[296,16,56]{0,2,1:T(8,128)}, u32[]{:S(2)}, u32[]{:S(2)}) async-start(f32[296,16,56]{0,2,1:T(8,128)} %fusion.7), calls=%async_computation.1 | async-start | bytes 2752512 | tf_op jit(solution)/shard_map/all_to_all | solution.py:28
  171.0 118.6 %all-gather.3.cloned.1.call-done = bf16[4096,896]{0,1:T(8,128)(2,1)} async-done(((bf16[128,896]{0,1:T(8,128)(2,1)}), bf16[4096,896]{0,1:T(8,128)(2,1)}) %all-gather.3.cloned.1.call-update) | async-done | bytes 7340048 | tf_op jit(solution)/shard_map/all_gather | solution.py:22
  289.6 5.8 %convolution_multiply_fusion.1 = f32[296,896]{1,0:T(8,128)S(1)} fusion(bf16[296,4096]{1,0:T(8,128)(2,1)S(1)} %copy-done, bf16[4096,896]{0,1:T(8,128)(2,1)} %all-gather.3.cloned.1.call-done), kind=kOutput, calls=%fused_computation.14 | convolution fusion | flops 2172914688 | bytes 10825728 | tf_op jit(solution)/shard_map/dot_general | solution.py:23
  295.4 1.6 copy.25
  297.0 3.6 %fusion.3 = f32[296,16,56]{0,2,1:T(8,128)} fusion(f32[296,16,56]{0,2,1:T(8,128)} %bitcast.40, bf16[296,16,2,56]{0,3,2,1:T(8,128)(2,1)} %bitcast.45, bf16[296,16,2,56]{0,3,2,1:T(8,128)(2,1)} %bitcast.43), kind=kLoop, calls=%fused_computation.5 | loop fusion | flops 2917376 | bytes 3182592 | tf_op jit(solution)/shard_map/div | solution.py:27
  300.6 0.0 all-to-all-done.1
  300.6 6.5 %all-to-all-start = ((f32[296,16,56]{0,2,1:T(8,128)}), f32[296,16,56]{0,2,1:T(8,128)}, u32[]{:S(2)}, u32[]{:S(2)}) async-start(f32[296,16,56]{0,2,1:T(8,128)} %fusion.3), calls=%async_computation | async-start | bytes 2752512 | tf_op jit(solution)/shard_map/all_to_all | solution.py:28
  307.1 1.4 reduce_sum.19
  308.5 0.0 copy-start.2
  308.6 17.9 %all-to-all-done = f32[296,16,56]{0,2,1:T(8,128)} async-done(((f32[296,16,56]{0,2,1:T(8,128)}), f32[296,16,56]{0,2,1:T(8,128)}, u32[]{:S(2)}, u32[]{:S(2)}) %all-to-all-start) | async-done | bytes 1060896 | tf_op jit(solution)/shard_map/all_to_all | solution.py:28
  326.4 1.4 reduce_sum.18
  327.9 0.1 copy.31
  328.0 0.0 copy-done.2
  328.0 0.7 multiply_add_fusion
  (3 shorter events, 0.0 us)
Async XLA Ops:
  6.5 146.8 %copy-start = (bf16[296,4096]{1,0:T(8,128)(2,1)S(1)}, bf16[296,4096]{1,0:T(8,128)(2,1)}, u32[]{:S(2)}) copy-start(bf16[296,4096]{1,0:T(8,128)(2,1)} %param.5) | copy-start | bytes 7274500
  6.5 146.8 %all-gather.5.cloned.1.call-start = ((), (), s32[]{:S(2)}) async-start(), calls=%async_computation.3 | async-start | bytes 7569408 | tf_op jit(solution)/shard_map/all_gather | solution.py:22
  8.8 3.2 copy-start.1
  8.8 280.8 %all-gather.3.cloned.1.call-start = ((), (), s32[]{:S(2)}) async-start(), calls=%async_computation.2 | async-start | bytes 7569408 | tf_op jit(solution)/shard_map/all_gather | solution.py:22
  164.5 136.2 %all-to-all-start.1 = ((f32[296,16,56]{0,2,1:T(8,128)}), f32[296,16,56]{0,2,1:T(8,128)}, u32[]{:S(2)}, u32[]{:S(2)}) async-start(f32[296,16,56]{0,2,1:T(8,128)} %fusion.7), calls=%async_computation.1 | async-start | bytes 2752512 | tf_op jit(solution)/shard_map/all_to_all | solution.py:28
  300.6 25.8 %all-to-all-start = ((f32[296,16,56]{0,2,1:T(8,128)}), f32[296,16,56]{0,2,1:T(8,128)}, u32[]{:S(2)}, u32[]{:S(2)}) async-start(f32[296,16,56]{0,2,1:T(8,128)} %fusion.3), calls=%async_computation | async-start | bytes 2752512 | tf_op jit(solution)/shard_map/all_to_all | solution.py:28
  308.5 19.5 %copy-start.2 = (bf16[296,112]{1,0:T(8,128)(2,1)S(1)}, bf16[296,112]{1,0:T(8,128)(2,1)}, u32[]{:S(2)}) copy-start(bf16[296,112]{1,0:T(8,128)(2,1)} %param.9) | copy-start | bytes 198916
Sparse Core Ops, SparseCore 0:
  10.4 142.8 all-gather.4
  156.4 133.1 all-gather.2

commit v4 on v2

--- a/solution.py
+++ b/solution.py
@@ -5,7 +5,8 @@
 
 
 def shards(hidden, cotangent, first_moment, second_moment, outer_momentum):
-    gathered = lax.all_gather(cotangent, "fsdp", axis=0, tiled=True)
+    flat = lax.all_gather(cotangent.reshape(-1), "fsdp", axis=0, tiled=True)
+    gathered = flat.reshape(-1, cotangent.shape[1])
     gradient = jnp.dot(hidden, gathered, preferred_element_type=jnp.float32) / gathered.shape[0]
     first_new = 0.9 * first_moment[0].astype(jnp.float32) + 0.1 * gradient
     second_new = 0.95 * second_moment[0].astype(jnp.float32) + 0.05 * gradient * gradient

time: 279 us -> 307 us (1.10)
  local copies, waits for them, and re-layouts: 6.42 us -> 36.3 us
    reshape x0 -> x2, local copies, waits for them, and re-layouts: none -> 29.8 us  [the longest x1 27.3 us: shards(): gathered = flat.reshape(-1, cotangent.shape[1])]
where the time goes in v4:
time: 307 us; the launch traced here: 306 us
  waiting for transfers between devices  182 us (59%)
  blocking collectives  59.1 us (19%)
  local copies, waits for them, and re-layouts  36.3 us (12%)
  between operations  13.4 us (4%)
  matrix products  12.2 us (4%)
    all_gather x1, waiting for transfers between devices, shards(): flat = lax.all_gather(cotangent.reshape(-1), 'fsdp', axis=0, tiled=True)  182 us
    all_to_all x1, blocking collectives, shards(): received = lax.all_to_all(blocks, 'worker', 1, 1, tiled=True)  59.1 us
    reshape x1, local copies, waits for them, and re-layouts, shards(): gathered = flat.reshape(-1, cotangent.shape[1])  27.3 us
    dot_general x1, matrix products, shards(): jnp.dot(hidden, gathered, preferred_element_type=jnp.float32)  12.2 us
    reshape x2, local copies, waits for them, and re-layouts, shards(): blocks = pseudo.reshape(rows, workers, cols // workers)  6.41 us
  transfers between devices with their start and end apart: 1, of which 1 were waited for; matrix products, arithmetic and copies ran while one was open for 0% of the time, Pallas kernels for 0%

profile of v4, /device:TPU:1, one launch (start us, length us, event | category | flops | bytes accessed | tf_op | source)
XLA Modules:
  0.0 305.8 jit_solution(17225887538212998928)
XLA Ops:
  6.5 0.0 copy-start
  6.5 0.0 all-gather.2.cloned.1.call-start
  6.5 2.5 reshape.15
  9.1 0.0 all-gather.2.cloned.1.call-update
  9.1 0.0 copy-start.2
  9.1 182.3 %all-gather.2.cloned.1.call-done = bf16[7340032]{0:T(1024)(128)(2,1)} async-done(((bf16[229376]{0:T(1024)(128)(2,1)}), bf16[7340032]{0:T(1024)(128)(2,1)}) %all-gather.2.cloned.1.call-update) | async-done | bytes 14680080 | tf_op jit(solution)/shard_map/all_gather | solution.py:8
  191.4 27.3 %reshape.16 = bf16[4096,1792]{1,0:T(8,128)(2,1)} reshape(bf16[7340032]{0:T(1024)(128)(2,1)} %all-gather.2.cloned.1.call-done) | data formatting | bytes 29360128 | tf_op jit(solution)/shard_map/reshape | solution.py:9
  218.7 0.0 copy-done
  218.7 0.0 copy-done.2
  218.7 12.2 %fusion.2 = f32[296,1792]{1,0:T(8,128)} fusion(bf16[1,296,1792]{2,1,0:T(8,128)(2,1)S(1)} %copy-done.2, bf16[1,296,1792]{2,1,0:T(8,128)(2,1)} %param.7, bf16[296,4096]{1,0:T(8,128)(2,1)S(1)} %copy-done, bf16[4096,1792]{1,0:T(8,128)(2,1)} %reshape.16), kind=kOutput, calls=%fused_computation.3 | convolution fusion | flops 4351664128 | bytes 21348352 | tf_op jit(solution)/shard_map/dot_general | solution.py:10
  230.9 3.9 %reshape.17 = f32[296,16,112]{2,1,0:T(8,128)} reshape(f32[296,1792]{1,0:T(8,128)} %fusion.2) | data formatting | bytes 4243456 | tf_op jit(solution)/shard_map/reshape | solution.py:16
  234.8 2.5 copy.6
  237.3 59.1 %all_to_all.5 = f32[296,16,112]{2,0,1:T(8,128)} all-to-all(f32[296,16,112]{2,0,1:T(8,128)S(1)} %copy.6), channel_id=1, replica_groups=mesh['worker'=16,'fsdp'=32] {'worker'}, dimensions={1} | all-to-all | bytes 4243456 | tf_op jit(solution)/shard_map/all_to_all | solution.py:17
  296.4 0.0 copy-start.1
  296.4 1.9 reduce_sum.9
  298.3 0.0 copy-done.1
  298.3 0.7 multiply_add_fusion
Async XLA Ops:
  6.5 212.2 %copy-start = (bf16[296,4096]{1,0:T(8,128)(2,1)S(1)}, bf16[296,4096]{1,0:T(8,128)(2,1)}, u32[]{:S(2)}) copy-start(bf16[296,4096]{1,0:T(8,128)(2,1)} %param.5) | copy-start | bytes 7274500
  6.5 184.8 %all-gather.2.cloned.1.call-start = ((), (), s32[]{:S(2)}) async-start(), calls=%async_computation.1 | async-start | bytes 15138816 | tf_op jit(solution)/shard_map/all_gather | solution.py:8
  9.1 209.6 %copy-start.2 = (bf16[1,296,1792]{2,1,0:T(8,128)(2,1)S(1)}, bf16[1,296,1792]{2,1,0:T(8,128)(2,1)}, u32[]{:S(2)}) copy-start(bf16[1,296,1792]{2,1,0:T(8,128)(2,1)} %param.8) | copy-start | bytes 3182596
  296.4 1.9 copy-start.1
Sparse Core Ops, SparseCore 0:
  10.5 180.7 all-gather.1

commit v5 on v0

v5 whole, which is shorter than its diff:
```python
import jax
import jax.numpy as jnp
from jax import lax
from jax.sharding import PartitionSpec as P


def shards(hidden, cotangent, first_moment, second_moment, outer_momentum):
    workers = lax.axis_size("worker")
    rows = hidden.shape[0]
    cols = cotangent.shape[1]
    gathered = lax.all_gather(cotangent, "fsdp", axis=0, tiled=True)
    tokens = gathered.shape[0]
    cut = (rows // 2 + 7) // 8 * 8
    m1, m2 = first_moment[0], second_moment[0]
    parts = []
    for lo, hi in ((0, cut), (cut, rows)):
        if parts:
            hidden, m1, m2, _ = lax.optimization_barrier((hidden, m1, m2, parts[-1]))
        gradient = jnp.dot(hidden[lo:hi], gathered, preferred_element_type=jnp.float32) / tokens
        first_new = 0.9 * m1[lo:hi].astype(jnp.float32) + 0.1 * gradient
        second_new = 0.95 * m2[lo:hi].astype(jnp.float32) + 0.05 * gradient * gradient
        pseudo = first_new / (jnp.sqrt(second_new) + 1e-08)
        blocks = pseudo.reshape(hi - lo, workers, cols // workers)
        received = lax.all_to_all(blocks, "worker", 1, 1, tiled=True)
        parts.append(received.sum(axis=1) / workers)
    average = jnp.concatenate(parts, axis=0)
    return 0.9 * outer_momentum.astype(jnp.float32) + average


def solution(mesh):
    in_specs = (
        P("fsdp", "worker"),
        P(("worker", "fsdp"), None),
        P("worker", "fsdp", None),
        P("worker", "fsdp", None),
        P("fsdp", "worker"),
    )
    out_specs = P("fsdp", "worker")
    return jax.shard_map(shards, mesh=mesh, in_specs=in_specs, out_specs=out_specs, check_vma=False)
```

time: 306 us -> 287 us (0.938)
  waiting for transfers between devices: 273 us -> 185 us
  blocking collectives: 0 us -> 67.4 us
  matrix products: 12.5 us -> 17 us
    unnamed x3 -> x1, waiting for transfers between devices: 89.4 us -> 0.71 us
    all_to_all x0 -> x2, blocking collectives: none -> 67.4 us  [shards(): received = lax.all_to_all(blocks, 'worker', 1, 1, tiled=True)]
    dot_general x1 -> x2, matrix products: 12.5 us -> 17 us  [shards(): jnp.dot(hidden[lo:hi], gathered, preferred_element_type=jnp.float32)]
    unnamed x6 -> x2, local copies, waits for them, and re-layouts: 4.24 us -> 0.78 us
  transfers between devices with their start and end apart: 2 -> 1, of which waited for: 2 -> 1; matrix products, arithmetic and copies ran while one was open for 0% -> 0% of each run, Pallas kernels for 0% -> 0%
where the time goes in v5:
time: 287 us
  waiting for transfers between devices  185 us (64%)
  blocking collectives  67.4 us (23%)
  matrix products  17 us (6%)
  between operations  13.5 us (5%)
  local copies, waits for them, and re-layouts  3.24 us (1%)
    all_gather x1, waiting for transfers between devices, shards(): gathered = lax.all_gather(cotangent, 'fsdp', axis=0, tiled=True)  184 us
    all_to_all x2, blocking collectives, shards(): received = lax.all_to_all(blocks, 'worker', 1, 1, tiled=True)  67.4 us
    dot_general x2, matrix products, shards(): jnp.dot(hidden[lo:hi], gathered, preferred_element_type=jnp.float32)  17 us
  transfers between devices with their start and end apart: 1, of which 1 were waited for; matrix products, arithmetic and copies ran while one was open for 0% of the time, Pallas kernels for 0%

profile of v5, /device:TPU:1, one launch (start us, length us, event | category | flops | bytes accessed | tf_op | source)
XLA Modules:
  0.0 286.8 jit_solution(17790312696836183544)
XLA Ops:
  6.5 0.0 all-gather.2.cloned.1.call-start
  6.5 0.7 all-gather.2.cloned.1.call-update
  7.3 184.1 %all-gather.2.cloned.1.call-done = bf16[4096,1792]{1,0:T(8,128)(2,1)} async-done(((bf16[128,1792]{1,0:T(8,128)(2,1)}), bf16[4096,1792]{1,0:T(8,128)(2,1)}) %all-gather.2.cloned.1.call-update) | async-done | bytes 14680080 | tf_op jit(solution)/shard_map/all_gather | solution.py:11
  191.3 8.6 %fusion.6 = f32[152,1792]{1,0:T(8,128)S(1)} fusion(bf16[4096,1792]{1,0:T(8,128)(2,1)} %all-gather.2.cloned.1.call-done, bf16[296,4096]{1,0:T(8,128)(2,1)} %param.5, bf16[1,296,1792]{2,1,0:T(8,128)(2,1)} %param.8, bf16[1,296,1792]{2,1,0:T(8,128)(2,1)} %param.7), kind=kOutput, calls=%fused_computation.7 | convolution fusion | flops 2234638336 | bytes 18104320 | tf_op jit(solution)/shard_map/dot_general | solution.py:19
  200.0 0.9 reshape.14
  200.8 0.4 copy.6
  201.2 46.7 %all_to_all.10 = f32[152,16,112]{2,0,1:T(8,128)S(1)} all-to-all(f32[152,16,112]{2,0,1:T(8,128)S(1)} %copy.6), channel_id=1, replica_groups=mesh['worker'=16,'fsdp'=32] {'worker'}, dimensions={1} | all-to-all | bytes 2179072 | tf_op jit(solution)/shard_map/all_to_all | solution.py:24
  248.0 0.1 reduce_sum.18
  248.1 8.4 %add_divide_fusion = f32[144,1792]{1,0:T(8,128)S(1)} fusion(bf16[4096,1792]{1,0:T(8,128)(2,1)} %all-gather.2.cloned.1.call-done, bf16[296,4096]{1,0:T(8,128)(2,1)} %param.5, bf16[296,1792]{1,0:T(8,128)(2,1)} %bitcast.16, bf16[296,1792]{1,0:T(8,128)(2,1)} %bitcast.17), kind=kOutput, calls=%fused_computation.9 | convolution fusion | flops 2117025792 | bytes 17924096 | tf_op jit(solution)/shard_map/dot_general | solution.py:19
  256.5 0.8 reshape.15
  257.3 0.4 copy.7
  257.7 20.6 %all_to_all.11 = f32[144,16,112]{2,0,1:T(8,128)S(1)} all-to-all(f32[144,16,112]{2,0,1:T(8,128)S(1)} %copy.7), channel_id=1, replica_groups=mesh['worker'=16,'fsdp'=32] {'worker'}, dimensions={1} | all-to-all | bytes 2064384 | tf_op jit(solution)/shard_map/all_to_all | solution.py:24
  278.4 0.0 copy-start
  278.4 0.1 reduce_sum.19
  278.5 0.8 copy-done
  279.2 0.7 maximum_add_fusion
  (2 shorter events, 0.0 us)
Async XLA Ops:
  6.5 184.8 %all-gather.2.cloned.1.call-start = ((), (), s32[]{:S(2)}) async-start(), calls=%async_computation.2 | async-start | bytes 15138816 | tf_op jit(solution)/shard_map/all_gather | solution.py:11
  278.4 0.9 copy-start
Sparse Core Ops, SparseCore 0:
  10.5 180.7 all-gather.1

commit v6 on v2

--- a/solution.py
+++ b/solution.py
@@ -12,9 +12,11 @@
     pseudo = first_new / (jnp.sqrt(second_new) + 1e-08)
     workers = lax.axis_size("worker")
     rows, cols = pseudo.shape
-    blocks = pseudo.reshape(rows, workers, cols // workers)
+    cut = rows // 4 // 8 * 8
+    offloaded = lax.psum_scatter(pseudo[:cut], "worker", scatter_dimension=1, tiled=True)
+    blocks = pseudo[cut:].reshape(rows - cut, workers, cols // workers)
     received = lax.all_to_all(blocks, "worker", 1, 1, tiled=True)
-    average = received.sum(axis=1) / workers
+    average = jnp.concatenate([offloaded, received.sum(axis=1)], axis=0) / workers
     return 0.9 * outer_momentum.astype(jnp.float32) + average
 
 

time: 279 us -> 317 us (1.14)
  waiting for transfers between devices: 185 us -> 248 us
  blocking collectives: 59.1 us -> 0 us
  starting transfers between devices: 0.01 us -> 29.2 us
  local copies, waits for them, and re-layouts: 6.42 us -> 11.5 us
    unnamed x1 -> x3, waiting for transfers between devices: 0.71 us -> 63.7 us
    all_to_all x1 -> x0, blocking collectives: 59.1 us -> none  [shards(): received = lax.all_to_all(blocks, 'worker', 1, 1, tiled=True)]
    all_to_all x0 -> x1, starting transfers between devices: none -> 29.2 us  [shards(): received = lax.all_to_all(blocks, 'worker', 1, 1, tiled=True)]
    unnamed x4 -> x8, local copies, waits for them, and re-layouts: 0.01 us -> 3.5 us
  transfers between devices with their start and end apart: 1 -> 3, of which waited for: 1 -> 2; matrix products, arithmetic and copies ran while one was open for 0% -> 1% of each run, Pallas kernels for 0% -> 0%
where the time goes in v6:
time: 317 us; the launch traced here: 315 us
  waiting for transfers between devices  248 us (78%)
  starting transfers between devices  29.2 us (9%)
  between operations  13.5 us (4%)
  local copies, waits for them, and re-layouts  11.5 us (4%)
  matrix products  11.2 us (4%)
    all_gather x1, waiting for transfers between devices, shards(): gathered = lax.all_gather(cotangent, 'fsdp', axis=0, tiled=True)  184 us
    unnamed x3, waiting for transfers between devices  63.7 us
    all_to_all x1, starting transfers between devices, shards(): received = lax.all_to_all(blocks, 'worker', 1, 1, tiled=True)  29.2 us
    dot_general x1, matrix products, shards(): jnp.dot(hidden, gathered, preferred_element_type=jnp.float32)  11.2 us
    reshape x2, local copies, waits for them, and re-layouts, shards(): blocks = pseudo[cut:].reshape(rows - cut, workers, cols // workers)  6.68 us
  transfers between devices with their start and end apart: 3, of which 2 were waited for; matrix products, arithmetic and copies ran while one was open for 1% of the time, Pallas kernels for 0%

profile of v6, /device:TPU:1, one launch (start us, length us, event | category | flops | bytes accessed | tf_op | source)
XLA Modules:
  0.0 315.5 jit_solution(1296063517313588824)
XLA Ops:
  6.5 0.0 copy-start
  6.5 0.0 all-gather.2.cloned.1.call-start
  6.5 0.7 all-gather.2.cloned.1.call-update
  7.3 184.1 %all-gather.2.cloned.1.call-done = bf16[4096,1792]{1,0:T(8,128)(2,1)} async-done(((bf16[128,1792]{1,0:T(8,128)(2,1)}), bf16[4096,1792]{1,0:T(8,128)(2,1)}) %all-gather.2.cloned.1.call-update) | async-done | bytes 14680080 | tf_op jit(solution)/shard_map/all_gather | solution.py:8
  191.4 0.0 copy-done
  191.4 11.2 %fusion.2 = f32[296,1792]{1,0:T(8,128)S(1)} fusion(bf16[1,296,1792]{2,1,0:T(8,128)(2,1)} %param.8, bf16[1,296,1792]{2,1,0:T(8,128)(2,1)} %param.7, bf16[296,4096]{1,0:T(8,128)(2,1)S(1)} %copy-done, bf16[4096,1792]{1,0:T(8,128)(2,1)} %all-gather.2.cloned.1.call-done), kind=kOutput, calls=%fused_computation.3 | convolution fusion | flops 4351664128 | bytes 21348352 | tf_op jit(solution)/shard_map/dot_general | solution.py:9
  202.5 0.0 copy-start.1
  202.5 1.3 copy-done.1
  203.9 1.3 slice.9
  205.2 3.4 %reshape.9 = f32[224,16,112]{2,1,0:T(8,128)} reshape(f32[224,1792]{1,0:T(8,128)} %slice.9) | data formatting | bytes 3211264 | tf_op jit(solution)/shard_map/reshape | solution.py:17
  208.5 3.3 %copy.6 = f32[224,16,112]{2,0,1:T(8,128)} copy(f32[224,16,112]{2,1,0:T(8,128)} %reshape.9) | data formatting | bytes 3211264 | tf_op jit(solution)/shard_map/reshape | solution.py:17
  211.8 0.0 slice-start
  211.8 29.2 %all-to-all-start = ((f32[224,16,112]{2,0,1:T(8,128)}), f32[224,16,112]{2,0,1:T(8,128)}, u32[]{:S(2)}, u32[]{:S(2)}) async-start(f32[224,16,112]{2,0,1:T(8,128)} %copy.6), calls=%async_computation | async-start | bytes 3670016 | tf_op jit(solution)/shard_map/all_to_all | solution.py:18
  241.0 0.0 reduce-scatter.4.cloned.1.call-start
  241.1 0.0 slice-done
  241.1 0.0 copy-start.2
  241.1 1.3 copy.7
  242.4 0.0 reduce-scatter.4.cloned.1.call-update
  242.4 63.0 %reduce-scatter.4.cloned.1.call-done = f32[112,72]{1,0:T(8,128)} async-done(((f32[1792,72]{1,0:T(8,128)}), f32[112,72]{1,0:T(8,128)}) %reduce-scatter.4.cloned.1.call-update) | async-done | bytes 32272
  305.4 0.9 copy.8
  306.3 0.0 all-to-all-done
  306.3 1.6 reduce_sum.9
  307.9 0.0 copy-done.2
  307.9 0.7 fusion.3
Async XLA Ops:
  6.5 184.8 %copy-start = (bf16[296,4096]{1,0:T(8,128)(2,1)S(1)}, bf16[296,4096]{1,0:T(8,128)(2,1)}, u32[]{:S(2)}) copy-start(bf16[296,4096]{1,0:T(8,128)(2,1)} %param.5) | copy-start | bytes 7274500
  6.5 184.8 %all-gather.2.cloned.1.call-start = ((), (), s32[]{:S(2)}) async-start(), calls=%async_computation.2 | async-start | bytes 15138816 | tf_op jit(solution)/shard_map/all_gather | solution.py:8
  202.5 1.3 copy-start.1
  211.8 29.2 %slice-start = ((f32[296,1792]{1,0:T(8,128)}), f32[72,1792]{1,0:T(8,128)S(1)}, s32[]{:S(2)}) async-start(f32[296,1792]{1,0:T(8,128)} %copy-done.1), calls=%async_computation.4 | async-start | bytes 1032192 | tf_op jit(solution)/shard_map/slice | solution.py:16
  211.8 94.4 %all-to-all-start = ((f32[224,16,112]{2,0,1:T(8,128)}), f32[224,16,112]{2,0,1:T(8,128)}, u32[]{:S(2)}, u32[]{:S(2)}) async-start(f32[224,16,112]{2,0,1:T(8,128)} %copy.6), calls=%async_computation | async-start | bytes 3670016 | tf_op jit(solution)/shard_map/all_to_all | solution.py:18
  241.0 64.3 %reduce-scatter.4.cloned.1.call-start = ((), (), s32[]{:S(2)}) async-start(), calls=%async_computation.3 | async-start | bytes 974848
  241.1 66.8 %copy-start.2 = (bf16[296,112]{1,0:T(8,128)(2,1)S(1)}, bf16[296,112]{1,0:T(8,128)(2,1)}, u32[]{:S(2)}) copy-start(bf16[296,112]{1,0:T(8,128)(2,1)} %param.9) | copy-start | bytes 198916
Sparse Core Ops, SparseCore 0:
  10.5 180.7 all-gather.1
  244.7 60.6 reduce-scatter.3

commit v7 on v1

v7 whole, which is shorter than its diff:
```python
import jax
import jax.numpy as jnp
from jax import lax
from jax.sharding import Mesh
from jax.sharding import PartitionSpec as P

W = ("wx", "wz", "wc")
F = ("fz", "fy")
SPLIT = {"worker": (4, 2, 2), "fsdp": (4, 8)}


def shards(hidden, cotangent, first_moment, second_moment, outer_momentum):
    gathered = lax.all_gather(cotangent, F, axis=0, tiled=True)
    gradient = jnp.dot(hidden, gathered, preferred_element_type=jnp.float32) / gathered.shape[0]
    first_new = 0.9 * first_moment[0].astype(jnp.float32) + 0.1 * gradient
    second_new = 0.95 * second_moment[0].astype(jnp.float32) + 0.05 * gradient * gradient
    pseudo = first_new / (jnp.sqrt(second_new) + 1e-08)
    rows, cols = pseudo.shape
    nx, nz, nc = SPLIT["worker"]
    blocks = pseudo.reshape(rows, nx, nz, nc, cols // (nx * nz * nc))
    blocks = lax.all_to_all(blocks, "wc", 3, 3, tiled=True).sum(axis=3)
    blocks = lax.all_to_all(blocks, "wz", 2, 2, tiled=True).sum(axis=2)
    blocks = lax.all_to_all(blocks, "wx", 1, 1, tiled=True).sum(axis=1)
    average = blocks / (nx * nz * nc)
    return 0.9 * outer_momentum.astype(jnp.float32) + average


def solution(mesh):
    fine = Mesh(mesh.devices.reshape(SPLIT["worker"] + SPLIT["fsdp"]), W + F)
    in_specs = (
        P(F, W),
        P(W + F, None),
        P(W, F, None),
        P(W, F, None),
        P(F, W),
    )
    out_specs = P(F, W)
    return jax.shard_map(shards, mesh=fine, in_specs=in_specs, out_specs=out_specs, check_vma=False)
```

time: 441 us -> 292 us (0.66)
  waiting for transfers between devices: 410 us -> 185 us
  blocking collectives: 0 us -> 61.1 us
  local copies, waits for them, and re-layouts: 4.23 us -> 12 us
  other arithmetic: 0.69 us -> 7.2 us
    all_gather x2 -> x1, waiting for transfers between devices: 323 us -> 184 us  [shards(): gathered = lax.all_gather(cotangent, F, axis=0, tiled=True)]
    unnamed x8 -> x1, waiting for transfers between devices: 87.1 us -> 0.71 us
    all_to_all x0 -> x3, blocking collectives: none -> 61.1 us  [the longest x1 24.6 us: shards(): blocks = lax.all_to_all(blocks, 'wc', 3, 3, tiled=True).sum(axis=3)]
    reshape x0 -> x2, local copies, waits for them, and re-layouts: none -> 10.4 us  [shards(): blocks = pseudo.reshape(rows, nx, nz, nc, cols // (nx * nz * nc))]
    reduce_sum x0 -> x3, other arithmetic: none -> 6.51 us  [the longest x1 4.69 us: shards(): blocks = lax.all_to_all(blocks, 'wc', 3, 3, tiled=True).sum(axis=3)]
  transfers between devices with their start and end apart: 5 -> 1, of which waited for: 5 -> 1; matrix products, arithmetic and copies ran while one was open for 0% -> 0% of each run, Pallas kernels for 0% -> 0%
where the time goes in v7:
time: 292 us; the launch traced here: 291 us
  waiting for transfers between devices  185 us (63%)
  blocking collectives  61.1 us (21%)
  between operations  13.4 us (5%)
  matrix products  12.5 us (4%)
  local copies, waits for them, and re-layouts  12 us (4%)
  other arithmetic  7.2 us (2%)
    all_gather x1, waiting for transfers between devices, shards(): gathered = lax.all_gather(cotangent, F, axis=0, tiled=True)  184 us
    all_to_all x1, blocking collectives, shards(): blocks = lax.all_to_all(blocks, 'wc', 3, 3, tiled=True).sum(axis=3)  24.6 us
    all_to_all x1, blocking collectives, shards(): blocks = lax.all_to_all(blocks, 'wz', 2, 2, tiled=True).sum(axis=2)  23.8 us
    all_to_all x1, blocking collectives, shards(): blocks = lax.all_to_all(blocks, 'wx', 1, 1, tiled=True).sum(axis=1)  12.7 us
    dot_general x1, matrix products, shards(): jnp.dot(hidden, gathered, preferred_element_type=jnp.float32)  12.5 us
    reshape x2, local copies, waits for them, and re-layouts, shards(): blocks = pseudo.reshape(rows, nx, nz, nc, cols // (nx * nz * nc))  10.4 us
  transfers between devices with their start and end apart: 1, of which 1 were waited for; matrix products, arithmetic and copies ran while one was open for 0% of the time, Pallas kernels for 0%

profile of v7, /device:TPU:1, one launch (start us, length us, event | category | flops | bytes accessed | tf_op | source)
XLA Modules:
  0.0 291.1 jit_solution(11330176598227712916)
XLA Ops:
  6.5 0.0 copy-start
  6.5 0.0 all-gather.2.cloned.1.call-start
  6.5 0.7 all-gather.2.cloned.1.call-update
  7.3 184.1 %all-gather.2.cloned.1.call-done = bf16[4096,1792]{1,0:T(8,128)(2,1)} async-done(((bf16[128,1792]{1,0:T(8,128)(2,1)}), bf16[4096,1792]{1,0:T(8,128)(2,1)}) %all-gather.2.cloned.1.call-update) | async-done | bytes 14680080 | tf_op jit(solution)/shard_map/all_gather | solution.py:13
  191.3 0.0 copy-done
  191.4 12.5 %fusion.2 = f32[296,1792]{1,0:T(8,128)} fusion(bf16[1,296,1792]{2,1,0:T(8,128)(2,1)} %param.8, bf16[1,296,1792]{2,1,0:T(8,128)(2,1)} %param.7, bf16[296,4096]{1,0:T(8,128)(2,1)S(1)} %copy-done, bf16[4096,1792]{1,0:T(8,128)(2,1)} %all-gather.2.cloned.1.call-done), kind=kOutput, calls=%fused_computation.3 | convolution fusion | flops 4351664128 | bytes 21348352 | tf_op jit(solution)/shard_map/dot_general | solution.py:14
  203.9 7.5 %reshape.9 = f32[296,4,2,2,112]{4,3,2,1,0:T(2,128)} reshape(f32[296,1792]{1,0:T(8,128)} %fusion.2) | data formatting | bytes 4243456 | tf_op jit(solution)/shard_map/reshape | solution.py:20
  211.3 2.9 %copy.7 = f32[296,4,2,2,112]{4,2,1,0,3:T(2,128)S(1)} copy(f32[296,4,2,2,112]{4,3,2,1,0:T(2,128)} %reshape.9) | data formatting | bytes 4243456 | tf_op jit(solution)/shard_map/reshape | solution.py:20
  214.3 24.6 %all_to_all.15 = f32[296,4,2,2,112]{4,2,1,0,3:T(2,128)} all-to-all(f32[296,4,2,2,112]{4,2,1,0,3:T(2,128)S(1)} %copy.7), channel_id=1, replica_groups=mesh['wx'=4,'wz'=2,'wc'=2,'fz'=4,'fy'=8] {'wc'}, dimensions={3} | all-to-all | bytes 4243456 | tf_op jit(solution)/shard_map/all_to_all | solution.py:21
  238.9 4.7 %reduce_sum.27 = f32[296,4,2,112]{3,2,1,0:T(2,128)} reduce(f32[296,4,2,2,112]{4,2,1,0,3:T(2,128)} %all_to_all.15, f32[]{:T(128)} %constant.19.clone.1), dimensions={3}, to_apply=%region_0.0 | reduce | flops 265216 | bytes 3182596 | tf_op jit(solution)/shard_map/reduce_sum | solution.py:21
  243.6 1.6 copy.8
  245.2 23.8 %all_to_all.16 = f32[296,4,2,112]{3,1,0,2:T(4,128)} all-to-all(f32[296,4,2,112]{3,1,0,2:T(4,128)S(1)} %copy.8), channel_id=1, replica_groups=mesh['wx'=4,'wz'=2,'wc'=2,'fz'=4,'fy'=8] {'wz'}, dimensions={2} | all-to-all | bytes 2121728 | tf_op jit(solution)/shard_map/all_to_all | solution.py:22
  269.0 0.0 copy-start.1
  269.0 1.8 reduce_sum.28
  270.8 12.7 %all_to_all.17 = f32[296,4,112]{2,0,1:T(8,128)S(1)} all-to-all(f32[296,4,112]{2,0,1:T(8,128)S(1)} %copy.9), channel_id=1, replica_groups=mesh['wx'=4,'wz'=2,'wc'=2,'fz'=4,'fy'=8] {'wx'}, dimensions={1} | all-to-all | bytes 1060864 | tf_op jit(solution)/shard_map/all_to_all | solution.py:23
  283.6 0.0 copy-done.1
  283.6 0.7 multiply_add_fusion
  (2 shorter events, 0.1 us)
Async XLA Ops:
  6.5 184.8 %copy-start = (bf16[296,4096]{1,0:T(8,128)(2,1)S(1)}, bf16[296,4096]{1,0:T(8,128)(2,1)}, u32[]{:S(2)}) copy-start(bf16[296,4096]{1,0:T(8,128)(2,1)} %param.5) | copy-start | bytes 7274500
  6.5 184.8 %all-gather.2.cloned.1.call-start = ((), (), s32[]{:S(2)}) async-start(), calls=%async_computation.3 | async-start | bytes 15138816 | tf_op jit(solution)/shard_map/all_gather | solution.py:13
  269.0 14.6 %copy-start.1 = (bf16[296,112]{1,0:T(8,128)(2,1)S(1)}, bf16[296,112]{1,0:T(8,128)(2,1)}, u32[]{:S(2)}) copy-start(bf16[296,112]{1,0:T(8,128)(2,1)} %param.9) | copy-start | bytes 198916
Sparse Core Ops, SparseCore 0:
  10.5 180.7 all-gather.1

commit v8 on v7

v8 whole, which is shorter than its diff:
```python
import jax
import jax.numpy as jnp
from jax import lax
from jax.sharding import Mesh
from jax.sharding import PartitionSpec as P

W = ("wx", "wz", "wc")
F = ("fz", "fy")
SPLIT = {"worker": (4, 2, 2), "fsdp": (4, 8)}


def shards(hidden, cotangent, first_moment, second_moment, outer_momentum):
    gathered = lax.all_gather(cotangent, ("fy", "fz"), axis=0, tiled=True)
    nz, ny = SPLIT["fsdp"]
    rows, tokens = hidden.shape
    reordered = hidden.reshape(rows, nz, ny, tokens // (nz * ny)).transpose(0, 2, 1, 3).reshape(rows, tokens)
    gradient = jnp.dot(reordered, gathered, preferred_element_type=jnp.float32) / gathered.shape[0]
    first_new = 0.9 * first_moment[0].astype(jnp.float32) + 0.1 * gradient
    second_new = 0.95 * second_moment[0].astype(jnp.float32) + 0.05 * gradient * gradient
    pseudo = first_new / (jnp.sqrt(second_new) + 1e-08)
    workers = lax.axis_size(W)
    cols = pseudo.shape[1]
    blocks = pseudo.reshape(rows, workers, cols // workers)
    received = lax.all_to_all(blocks, W, 1, 1, tiled=True)
    average = received.sum(axis=1) / workers
    return 0.9 * outer_momentum.astype(jnp.float32) + average


def solution(mesh):
    fine = Mesh(mesh.devices.reshape(SPLIT["worker"] + SPLIT["fsdp"]), W + F)
    in_specs = (
        P(F, W),
        P(W + F, None),
        P(W, F, None),
        P(W, F, None),
        P(F, W),
    )
    out_specs = P(F, W)
    return jax.shard_map(shards, mesh=fine, in_specs=in_specs, out_specs=out_specs, check_vma=False)
```

time: 292 us -> 276 us (0.945)
  waiting for transfers between devices: 185 us -> 178 us
  other arithmetic: 7.2 us -> 0.86 us
    all_gather x1, waiting for transfers between devices: 184 us -> 177 us  [shards(): gathered = lax.all_gather(cotangent, ('fy', 'fz'), axis=0, tiled=True)]
    reduce_sum x3 -> x1, other arithmetic: 6.51 us -> 0.17 us  [shards(): average = received.sum(axis=1) / workers]
    unnamed x4 -> x5, local copies, waits for them, and re-layouts: 0.01 us -> 2.94 us
    reshape x2 -> x4, local copies, waits for them, and re-layouts: 10.4 us -> 8.27 us  [the longest x2 4.48 us: shards(): hidden.reshape(rows, nz, ny, tokens // (nz * ny)).transpose(0, 2, 1, 3)]
    all_to_all x3 -> x1, blocking collectives: 61.1 us -> 59 us  [shards(): received = lax.all_to_all(blocks, W, 1, 1, tiled=True)]
  transfers between devices with their start and end apart: 1 -> 1, of which waited for: 1 -> 1; matrix products, arithmetic and copies ran while one was open for 0% -> 2% of each run, Pallas kernels for 0% -> 0%
where the time goes in v8:
time: 276 us; the launch traced here: 275 us
  waiting for transfers between devices  178 us (64%)
  blocking collectives  59 us (21%)
  between operations  13.4 us (5%)
  matrix products  12.9 us (5%)
  local copies, waits for them, and re-layouts  11.2 us (4%)
    all_gather x1, waiting for transfers between devices, shards(): gathered = lax.all_gather(cotangent, ('fy', 'fz'), axis=0, tiled=True)  177 us
    all_to_all x1, blocking collectives, shards(): received = lax.all_to_all(blocks, W, 1, 1, tiled=True)  59 us
    dot_general x1, matrix products, shards(): jnp.dot(reordered, gathered, preferred_element_type=jnp.float32)  12.9 us
  transfers between devices with their start and end apart: 1, of which 1 were waited for; matrix products, arithmetic and copies ran while one was open for 2% of the time, Pallas kernels for 0%

profile of v8, /device:TPU:1, one launch (start us, length us, event | category | flops | bytes accessed | tf_op | source)
XLA Modules:
  0.0 275.4 jit_solution(3912588997436417546)
XLA Ops:
  6.5 0.0 all-gather.2.cloned.1.call-start
  6.5 0.7 all-gather.2.cloned.1.call-update
  7.3 2.2 copy.9
  9.5 1.2 copy.11
  10.7 0.0 copy-start.1
  10.7 3.2 %reshape.16 = bf16[296,4096]{1,0:T(8,128)(2,1)} reshape(bf16[296,8,4,128]{3,2,1,0:T(4,128)(2,1)S(1)} %bitcast.20) | data formatting | bytes 4849664 | tf_op jit(solution)/shard_map/reshape | solution.py:16
  14.0 177.4 %all-gather.2.cloned.1.call-done = bf16[4096,1792]{1,0:T(8,128)(2,1)} async-done(((bf16[128,1792]{1,0:T(8,128)(2,1)}), bf16[4096,1792]{1,0:T(8,128)(2,1)}) %all-gather.2.cloned.1.call-update) | async-done | bytes 14680080 | tf_op jit(solution)/shard_map/all_gather | solution.py:13
  191.3 0.0 copy-done.1
  191.3 12.9 %fusion.2 = f32[296,1792]{1,0:T(8,128)} fusion(bf16[1,296,1792]{2,1,0:T(8,128)(2,1)S(1)} %copy-done.1, bf16[1,296,1792]{2,1,0:T(8,128)(2,1)} %param.7, bf16[296,4096]{1,0:T(8,128)(2,1)} %reshape.16, bf16[4096,1792]{1,0:T(8,128)(2,1)} %all-gather.2.cloned.1.call-done), kind=kOutput, calls=%fused_computation.4 | convolution fusion | flops 4351664128 | bytes 21348352 | tf_op jit(solution)/shard_map/dot_general | solution.py:17
  204.2 3.0 %reshape.17 = f32[296,16,112]{2,1,0:T(8,128)S(1)} reshape(f32[296,1792]{1,0:T(8,128)} %fusion.2) | data formatting | bytes 4243456 | tf_op jit(solution)/shard_map/reshape | solution.py:23
  207.2 0.8 copy.8
  208.0 59.0 %all_to_all.5 = f32[296,16,112]{2,0,1:T(8,128)S(1)} all-to-all(f32[296,16,112]{2,0,1:T(8,128)S(1)} %copy.8), channel_id=1, replica_groups=mesh['wx'=4,'wz'=2,'wc'=2,'fz'=4,'fy'=8] {'wx','wz','wc'}, dimensions={1} | all-to-all | bytes 4243456 | tf_op jit(solution)/shard_map/all_to_all | solution.py:24
  267.0 0.0 copy-start
  267.0 0.2 reduce_sum.9
  267.2 0.7 copy-done
  267.9 0.7 multiply_add_fusion
Async XLA Ops:
  6.5 184.8 %all-gather.2.cloned.1.call-start = ((), (), s32[]{:S(2)}) async-start(), calls=%async_computation.1 | async-start | bytes 15138816 | tf_op jit(solution)/shard_map/all_gather | solution.py:13
  10.7 180.6 %copy-start.1 = (bf16[1,296,1792]{2,1,0:T(8,128)(2,1)S(1)}, bf16[1,296,1792]{2,1,0:T(8,128)(2,1)}, u32[]{:S(2)}) copy-start(bf16[1,296,1792]{2,1,0:T(8,128)(2,1)} %param.8) | copy-start | bytes 3182596
  267.0 0.9 copy-start
Sparse Core Ops, SparseCore 0:
  10.5 180.7 all-gather.1

commit v9 on v8

--- a/solution.py
+++ b/solution.py
@@ -15,14 +15,18 @@
     rows, tokens = hidden.shape
     reordered = hidden.reshape(rows, nz, ny, tokens // (nz * ny)).transpose(0, 2, 1, 3).reshape(rows, tokens)
     gradient = jnp.dot(reordered, gathered, preferred_element_type=jnp.float32) / gathered.shape[0]
-    first_new = 0.9 * first_moment[0].astype(jnp.float32) + 0.1 * gradient
-    second_new = 0.95 * second_moment[0].astype(jnp.float32) + 0.05 * gradient * gradient
+    gradient = lax.optimization_barrier(gradient)
+    workers = lax.axis_size(W)
+    cols = gradient.shape[1]
+
+    def blocked(x):
+        return x.reshape(rows, workers, cols // workers).transpose(1, 0, 2)
+
+    first_new = 0.9 * blocked(first_moment[0]).astype(jnp.float32) + 0.1 * blocked(gradient)
+    second_new = 0.95 * blocked(second_moment[0]).astype(jnp.float32) + 0.05 * blocked(gradient) * blocked(gradient)
     pseudo = first_new / (jnp.sqrt(second_new) + 1e-08)
-    workers = lax.axis_size(W)
-    cols = pseudo.shape[1]
-    blocks = pseudo.reshape(rows, workers, cols // workers)
-    received = lax.all_to_all(blocks, W, 1, 1, tiled=True)
-    average = received.sum(axis=1) / workers
+    received = lax.all_to_all(pseudo, W, 0, 0, tiled=True)
+    average = received.sum(axis=0) / workers
     return 0.9 * outer_momentum.astype(jnp.float32) + average
 
 

time: 276 us -> 279 us (1.011)
  waiting for transfers between devices: 178 us -> 168 us
  local copies, waits for them, and re-layouts: 11.2 us -> 19.2 us
  other arithmetic: 0.86 us -> 7.44 us
    all_gather x1, waiting for transfers between devices: 177 us -> 167 us  [shards(): gathered = lax.all_gather(cotangent, ('fy', 'fz'), axis=0, tiled=True)]
    mul x0 -> x2, local copies, waits for them, and re-layouts: none -> 7.02 us  [the longest x1 3.92 us: shards(): 0.95 * blocked(second_moment[0]).astype(jnp.float32)]
    div x0 -> x1, other arithmetic: none -> 3.59 us  [shards(): pseudo = first_new / (jnp.sqrt(second_new) + 1e-08)]
    mul x0 -> x2, other arithmetic: none -> 2.99 us  [the longest x1 1.5 us: shards(): 0.9 * blocked(first_moment[0]).astype(jnp.float32) + 0.1 * blocked(gradient)]
  transfers between devices with their start and end apart: 1 -> 1, of which waited for: 1 -> 1; matrix products, arithmetic and copies ran while one was open for 2% -> 6% of each run, Pallas kernels for 0% -> 0%
where the time goes in v9:
time: 279 us
  waiting for transfers between devices  168 us (60%)
  blocking collectives  59 us (21%)
  local copies, waits for them, and re-layouts  19.2 us (7%)
  between operations  13.4 us (5%)
  matrix products  11.8 us (4%)
  other arithmetic  7.44 us (3%)
    all_gather x1, waiting for transfers between devices, shards(): gathered = lax.all_gather(cotangent, ('fy', 'fz'), axis=0, tiled=True)  167 us
    all_to_all x1, blocking collectives, shards(): received = lax.all_to_all(pseudo, W, 0, 0, tiled=True)  59 us
    dot_general x1, matrix products, shards(): jnp.dot(reordered, gathered, preferred_element_type=jnp.float32)  11.8 us
  transfers between devices with their start and end apart: 1, of which 1 were waited for; matrix products, arithmetic and copies ran while one was open for 6% of the time, Pallas kernels for 0%

profile of v9, /device:TPU:1, one launch (start us, length us, event | category | flops | bytes accessed | tf_op | source)
XLA Modules:
  0.0 278.9 jit_solution(6060090076825661545)
XLA Ops:
  6.5 0.0 all-gather.2.cloned.1.call-start
  6.5 0.7 all-gather.2.cloned.1.call-update
  7.3 2.2 copy.11
  9.5 1.2 copy.13
  10.7 0.0 copy-start
  10.7 3.2 %reshape.18 = bf16[296,4096]{1,0:T(8,128)(2,1)} reshape(bf16[296,8,4,128]{3,2,1,0:T(4,128)(2,1)S(1)} %bitcast.19) | data formatting | bytes 4849664 | tf_op jit(solution)/shard_map/reshape | solution.py:16
  14.0 0.0 copy-done
  14.0 1.5 convert_multiply_fusion.1
  15.5 0.0 copy-start.1
  15.5 3.1 %mul.49 = f32[296,16,112]{2,1,0:T(8,128)S(1)} reshape(f32[1,296,1792]{2,1,0:T(8,128)} %convert_multiply_fusion.1) | data formatting | bytes 4243456 | tf_op jit(solution)/shard_map/mul | solution.py:25
  18.6 0.0 copy-done.1
  18.6 1.5 convert_multiply_fusion
  20.1 3.9 %mul.55 = f32[296,16,112]{2,1,0:T(8,128)} reshape(f32[1,296,1792]{2,1,0:T(8,128)} %convert_multiply_fusion) | data formatting | bytes 4243456 | tf_op jit(solution)/shard_map/mul | solution.py:26
  24.0 167.3 %all-gather.2.cloned.1.call-done = bf16[4096,1792]{1,0:T(8,128)(2,1)} async-done(((bf16[128,1792]{1,0:T(8,128)(2,1)}), bf16[4096,1792]{1,0:T(8,128)(2,1)}) %all-gather.2.cloned.1.call-update) | async-done | bytes 14680080 | tf_op jit(solution)/shard_map/all_gather | solution.py:13
  191.3 11.8 %convolution_multiply_fusion = f32[296,1792]{1,0:T(8,128)} fusion(bf16[296,4096]{1,0:T(8,128)(2,1)} %reshape.18, bf16[4096,1792]{1,0:T(8,128)(2,1)} %all-gather.2.cloned.1.call-done), kind=kOutput, calls=%fused_computation.1 | convolution fusion | flops 4345829376 | bytes 19226624 | tf_op jit(solution)/shard_map/dot_general | solution.py:17
  203.1 3.9 %reshape.19 = f32[296,16,112]{2,1,0:T(8,128)} reshape(f32[296,1792]{1,0:T(8,128)} %convolution_multiply_fusion) | data formatting | bytes 4243456 | tf_op jit(solution)/shard_map/reshape | solution.py:23
  207.1 3.6 %fusion.3 = f32[16,296,112]{2,0,1:T(8,128)S(1)} fusion(f32[296,16,112]{2,1,0:T(8,128)} %mul.55, f32[296,16,112]{2,1,0:T(8,128)} %reshape.19, f32[296,16,112]{2,1,0:T(8,128)S(1)} %mul.49), kind=kLoop, calls=%fused_computation.5 | loop fusion | flops 3713024 | bytes 8486912 | tf_op jit(solution)/shard_map/div | solution.py:27
  210.7 0.8 copy.10
  211.5 59.0 %all_to_all.5 = f32[16,296,112]{2,1,0:T(8,128)S(1)} all-to-all(f32[16,296,112]{2,1,0:T(8,128)S(1)} %copy.10), channel_id=1, replica_groups=mesh['wx'=4,'wz'=2,'wc'=2,'fz'=4,'fy'=8] {'wx','wz','wc'}, dimensions={0} | all-to-all | bytes 4243456 | tf_op jit(solution)/shard_map/all_to_all | solution.py:28
  270.5 0.0 copy-start.2
  270.5 0.2 reduce_sum.9
  270.6 0.7 copy-done.2
  271.3 0.7 multiply_add_fusion
Async XLA Ops:
  6.5 184.8 %all-gather.2.cloned.1.call-start = ((), (), s32[]{:S(2)}) async-start(), calls=%async_computation.1 | async-start | bytes 15138816 | tf_op jit(solution)/shard_map/all_gather | solution.py:13
  10.7 3.3 %copy-start = (bf16[1,296,1792]{2,1,0:T(8,128)(2,1)S(1)}, bf16[1,296,1792]{2,1,0:T(8,128)(2,1)}, u32[]{:S(2)}) copy-start(bf16[1,296,1792]{2,1,0:T(8,128)(2,1)} %param.7) | copy-start | bytes 3182596
  15.5 3.1 %copy-start.1 = (bf16[1,296,1792]{2,1,0:T(8,128)(2,1)S(1)}, bf16[1,296,1792]{2,1,0:T(8,128)(2,1)}, u32[]{:S(2)}) copy-start(bf16[1,296,1792]{2,1,0:T(8,128)(2,1)} %param.8) | copy-start | bytes 3182596
  270.5 0.9 copy-start.2
Sparse Core Ops, SparseCore 0:
  10.5 180.7 all-gather.1

commit v10 on v8

--- a/solution.py
+++ b/solution.py
@@ -20,8 +20,10 @@
     pseudo = first_new / (jnp.sqrt(second_new) + 1e-08)
     workers = lax.axis_size(W)
     cols = pseudo.shape[1]
-    blocks = pseudo.reshape(rows, workers, cols // workers)
-    received = lax.all_to_all(blocks, W, 1, 1, tiled=True)
+    nx, nz, nc = SPLIT["worker"]
+    blocks = pseudo.reshape(rows, nx, nz, nc, cols // workers).transpose(0, 3, 2, 1, 4)
+    blocks = blocks.reshape(rows, workers, cols // workers)
+    received = lax.all_to_all(blocks, W[::-1], 1, 1, tiled=True)
     average = received.sum(axis=1) / workers
     return 0.9 * outer_momentum.astype(jnp.float32) + average
 

time: 276 us -> 280 us (1.014)
  local copies, waits for them, and re-layouts: 11.2 us -> 14.8 us
    reshape x2, local copies, waits for them, and re-layouts: 3.79 us -> 7.39 us  [shards(): pseudo.reshape(rows, nx, nz, nc, cols // workers).transpose(0, 3, 2, 1, 4)]
where the time goes in v10:
time: 280 us
  waiting for transfers between devices  178 us (64%)
  blocking collectives  59.8 us (21%)
  local copies, waits for them, and re-layouts  14.8 us (5%)
  between operations  13.4 us (5%)
  matrix products  12.9 us (5%)
    all_gather x1, waiting for transfers between devices, shards(): gathered = lax.all_gather(cotangent, ('fy', 'fz'), axis=0, tiled=True)  177 us
    all_to_all x1, blocking collectives, shards(): received = lax.all_to_all(blocks, W[::-1], 1, 1, tiled=True)  59.8 us
    dot_general x1, matrix products, shards(): jnp.dot(reordered, gathered, preferred_element_type=jnp.float32)  12.9 us
    reshape x2, local copies, waits for them, and re-layouts, shards(): pseudo.reshape(rows, nx, nz, nc, cols // workers).transpose(0, 3, 2, 1, 4)  7.39 us
  transfers between devices with their start and end apart: 1, of which 1 were waited for; matrix products, arithmetic and copies ran while one was open for 2% of the time, Pallas kernels for 0%

profile of v10, /device:TPU:1, one launch (start us, length us, event | category | flops | bytes accessed | tf_op | source)
XLA Modules:
  0.0 279.8 jit_solution(17182858271387583749)
XLA Ops:
  6.5 0.0 all-gather.2.cloned.1.call-start
  6.5 0.7 all-gather.2.cloned.1.call-update
  7.3 2.2 copy.8
  9.5 1.2 copy.10
  10.7 0.0 copy-start.1
  10.7 3.2 %reshape.19 = bf16[296,4096]{1,0:T(8,128)(2,1)} reshape(bf16[296,8,4,128]{3,2,1,0:T(4,128)(2,1)S(1)} %bitcast.23) | data formatting | bytes 4849664 | tf_op jit(solution)/shard_map/reshape | solution.py:16
  14.0 177.4 %all-gather.2.cloned.1.call-done = bf16[4096,1792]{1,0:T(8,128)(2,1)} async-done(((bf16[128,1792]{1,0:T(8,128)(2,1)}), bf16[4096,1792]{1,0:T(8,128)(2,1)}) %all-gather.2.cloned.1.call-update) | async-done | bytes 14680080 | tf_op jit(solution)/shard_map/all_gather | solution.py:13
  191.3 0.0 copy-done.1
  191.3 12.9 %fusion.2 = f32[296,1792]{1,0:T(8,128)} fusion(bf16[1,296,1792]{2,1,0:T(8,128)(2,1)S(1)} %copy-done.1, bf16[1,296,1792]{2,1,0:T(8,128)(2,1)} %param.7, bf16[296,4096]{1,0:T(8,128)(2,1)} %reshape.19, bf16[4096,1792]{1,0:T(8,128)(2,1)} %all-gather.2.cloned.1.call-done), kind=kOutput, calls=%fused_computation.4 | convolution fusion | flops 4351664128 | bytes 21348352 | tf_op jit(solution)/shard_map/dot_general | solution.py:17
  204.2 6.6 %reshape.20 = f32[296,4,2,2,112]{4,3,2,1,0:T(2,128)S(1)} reshape(f32[296,1792]{1,0:T(8,128)} %fusion.2) | data formatting | bytes 4243456 | tf_op jit(solution)/shard_map/reshape | solution.py:24
  210.8 0.8 copy.7
  211.6 59.8 %all_to_all.5 = f32[296,16,112]{2,0,1:T(8,128)S(1)} all-to-all(f32[296,16,112]{2,0,1:T(8,128)S(1)} %bitcast.24), channel_id=1, replica_groups=mesh['wx'=4,'wz'=2,'wc'=2,'fz'=4,'fy'=8] {'wc','wz','wx'}, dimensions={1} | all-to-all | bytes 4243456 | tf_op jit(solution)/shard_map/all_to_all | solution.py:26
  271.4 0.0 copy-start
  271.4 0.2 reduce_sum.9
  271.5 0.7 copy-done
  272.3 0.7 multiply_add_fusion
Async XLA Ops:
  6.5 184.8 %all-gather.2.cloned.1.call-start = ((), (), s32[]{:S(2)}) async-start(), calls=%async_computation.1 | async-start | bytes 15138816 | tf_op jit(solution)/shard_map/all_gather | solution.py:13
  10.7 180.6 %copy-start.1 = (bf16[1,296,1792]{2,1,0:T(8,128)(2,1)S(1)}, bf16[1,296,1792]{2,1,0:T(8,128)(2,1)}, u32[]{:S(2)}) copy-start(bf16[1,296,1792]{2,1,0:T(8,128)(2,1)} %param.8) | copy-start | bytes 3182596
  271.4 0.9 copy-start
Sparse Core Ops, SparseCore 0:
  10.5 180.7 all-gather.1
